TPU v7x, 512 devices: a whole 4x8x8 slice. The times are simulated.
512 devices in a mesh: req: 128 (over y, z, core), tp: 4 (over x).
Axes of the slice: x: 4, y: 8, z: 8, core: 2. Of those that a mesh axis runs over, the one named last changes fastest.
Arguments:
- tokens: bfloat16 [65536, 1024], P('req', 'tp')
- placement: int32 [16384], P('req'), may hold values from 0 to 16383, as said below
- cache_len: int32 [256], P('req'), may hold values from 0 to 1024, as said below
- w_query: bfloat16 [1024, 1024], P(None, 'tp'), may hold values from -0.1875 to 0.1875
- w_key: bfloat16 [1024, 1024], P(None, 'tp'), may hold values from -0.1875 to 0.1875
- w_value: bfloat16 [1024, 1024], P(None, 'tp'), may hold values from -0.1875 to 0.1875
- w_out: bfloat16 [1024, 1024], P('tp'), may hold values from -0.1875 to 0.1875
- k_cache: bfloat16 [256, 1024, 1024], P('req', None, 'tp'), may hold values from -6 to 6
- v_cache: bfloat16 [256, 1024, 1024], P('req', None, 'tp'), may hold values from -6 to 6
- ln_gain: float32 [1024], replicated, may hold values from 0.1 to 1.9
- ln_bias: float32 [1024], replicated, may hold values from -0.5 to 0.5
Outputs:
- mixed: bfloat16 [65536, 1024], P('req', 'tp')
Inputs may be any that keep to these rules, and one draw needn't show every extreme that they name: `placement`: A permutation of the blocks. Of the 128 blocks that arrive on index s of req, exactly one goes to the owner range of every index t of req, and it lands at owner position t * 128 + s. `cache_len`: some request has exactly 1024 cached positions.
All inputs are finite; a program needn't handle non-finite values.
Results may differ from a plain program's by a relative error of at most 0.014.
The roundings to bfloat16 on the way count: a program that leaves them out, or rounds other values in their place, can miss the bound.
Values may be sent and summed in bfloat16 or wider, within the bound.
No kernel may reach another device: no remote copies, remote signals or barrier semaphores. Data moves between devices by JAX's collectives and lax.ppermute only.
A program may use at most 64 MiB of HBM per device.

v0:
```python
import jax
import jax.numpy as jnp
from jax import lax
from jax.sharding import PartitionSpec as P

D = 1024
HEADS = 16


def head_view(array, head_size):
    return array.reshape(array.shape[0], array.shape[1] // head_size, head_size)


def attend_padded(queries, new_keys, new_values, cache_keys, cache_values, length):
    head_size = D // HEADS
    new_count = queries.shape[0]
    span = cache_keys.shape[0]
    keys_all = head_view(jnp.concatenate([cache_keys, new_keys], 0), head_size)
    values_all = head_view(jnp.concatenate([cache_values, new_values], 0), head_size)
    query_heads = head_view(queries, head_size)
    scores = jnp.einsum(
        "qhd,khd->hqk", query_heads, keys_all, preferred_element_type=jnp.float32
    ) * head_size ** (-0.5)
    key_pos = jnp.arange(span + new_count, dtype=jnp.int32)[None, :]
    query_pos = jnp.arange(new_count, dtype=jnp.int32)[:, None]
    valid = jnp.where(key_pos < span, key_pos < length, key_pos - span <= query_pos)
    scores = jnp.where(valid[None], scores, -jnp.inf)
    top = jnp.max(scores, axis=-1, keepdims=True)
    weight = jnp.where(valid[None], jnp.exp(scores - top), 0.0)
    total = jnp.sum(weight, axis=-1)
    context = jnp.einsum(
        "hqk,khd->qhd", weight.astype(jnp.bfloat16), values_all, preferred_element_type=jnp.float32
    )
    context = context / jnp.transpose(total)[:, :, None]
    return context.reshape(new_count, queries.shape[1]).astype(jnp.bfloat16)


def attend_all(queries, new_keys, new_values, k_cache, v_cache, cache_len):
    request_count = k_cache.shape[0]
    req_shape = (request_count, queries.shape[0] // request_count, queries.shape[1])
    context = lax.map(
        lambda items: attend_padded(*items),
        (
            queries.reshape(req_shape),
            new_keys.reshape(req_shape),
            new_values.reshape(req_shape),
            k_cache,
            v_cache,
            cache_len,
        ),
    )
    return context.reshape(queries.shape)


def project_rows(whole, w_query, w_key, w_value):
    queries = jnp.dot(whole, w_query, preferred_element_type=jnp.float32).astype(jnp.bfloat16)
    new_keys = jnp.dot(whole, w_key, preferred_element_type=jnp.float32).astype(jnp.bfloat16)
    new_values = jnp.dot(whole, w_value, preferred_element_type=jnp.float32).astype(jnp.bfloat16)
    return (queries, new_keys, new_values)


def finish_rows(context, local, w_out, ln_gain, ln_bias):
    row_count, feat_width = local.shape
    partial_sum = jnp.dot(context, w_out, preferred_element_type=jnp.float32)
    attended = lax.psum_scatter(
        partial_sum.astype(jnp.bfloat16), "tp", scatter_dimension=1, tiled=True
    ).astype(jnp.float32)
    summed = local.astype(jnp.float32) + attended
    first_sum, square_sum = lax.psum(
        (jnp.sum(summed, axis=1), jnp.sum(summed * summed, axis=1)), "tp"
    )
    row_mean = first_sum / D
    row_var = square_sum / D - row_mean * row_mean
    offset = lax.axis_index("tp") * feat_width
    gain_part = lax.dynamic_slice_in_dim(ln_gain, offset, feat_width, 0)
    bias_part = lax.dynamic_slice_in_dim(ln_bias, offset, feat_width, 0)
    scaled = (summed - row_mean[:, None]) / jnp.sqrt(row_var[:, None] + 1e-05)
    return (scaled * gain_part + bias_part).astype(jnp.bfloat16)


def shards(
    tokens, placement, cache_len, w_query, w_key, w_value, w_out, k_cache, v_cache, ln_gain, ln_bias
):
    row_count, feat_width = tokens.shape
    block_count = placement.shape[0]
    block_rows = row_count // block_count
    per_peer = block_count // lax.axis_size("req")
    send_slot = placement // block_count * per_peer + placement % per_peer
    send_order = (
        jnp.zeros((block_count,), jnp.int32)
        .at[send_slot]
        .set(jnp.arange(block_count, dtype=jnp.int32))
    )

    def to_blocks(array):
        return array.reshape(block_count, block_rows, array.shape[1])

    arrived = lax.all_to_all(
        to_blocks(tokens)[send_order], "req", split_axis=0, concat_axis=0, tiled=True
    ).reshape(row_count, feat_width)
    whole = lax.all_gather(arrived, "tp", axis=1, tiled=True)
    queries, new_keys, new_values = project_rows(whole, w_query, w_key, w_value)
    context = attend_all(queries, new_keys, new_values, k_cache, v_cache, cache_len)
    normed = finish_rows(context, arrived, w_out, ln_gain, ln_bias)
    returned = lax.all_to_all(to_blocks(normed), "req", split_axis=0, concat_axis=0, tiled=True)
    return returned[send_slot].reshape(row_count, feat_width)


def solution(mesh):
    in_specs = (
        P("req", "tp"),
        P("req"),
        P("req"),
        P(None, "tp"),
        P(None, "tp"),
        P(None, "tp"),
        P("tp", None),
        P("req", None, "tp"),
        P("req", None, "tp"),
        P(),
        P(),
    )
    out_specs = P("req", "tp")
    return jax.shard_map(shards, mesh=mesh, in_specs=in_specs, out_specs=out_specs, check_vma=False)
```

profile of v0, /device:TPU:2, one launch (start us, length us, event | category | flops | bytes accessed | tf_op | source)
XLA Modules:
  0.0 176.9 jit_solution(9790313830979759242)
XLA Ops:
  6.5 0.7 compare_select_fusion.1
  7.3 1.0 scatter_custom_fusion
  8.3 1.0 reshape.143
  9.3 0.8 gather_fusion
  10.1 32.7 %all_to_all.10 = bf16[128,4,256]{2,1,0:T(4,128)(2,1)S(1)} all-to-all(bf16[128,4,256]{2,1,0:T(4,128)(2,1)S(1)} %gather_fusion), channel_id=1, replica_groups=mesh['req'=128,'tp'=4] {'req'}, dimensions={0} | all-to-all | bytes 524288 | tf_op jit(solution)/shard_map/all_to_all | solution.py:98
  42.8 0.8 reshape.144
  43.7 22.3 %all-gather.2.cloned.1.call-done = bf16[512,1024]{1,0:T(8,128)(2,1)} async-done(((bf16[512,256]{1,0:T(8,128)(2,1)}), bf16[512,1024]{1,0:T(8,128)(2,1)}) %all-gather.2.cloned.1.call-update) | async-done | bytes 1048592 | tf_op jit(solution)/shard_map/all_gather | solution.py:101
  66.0 2.5 %convolution_convert_fusion.2 = bf16[512,256]{1,0:T(8,128)(2,1)} fusion(bf16[512,1024]{1,0:T(8,128)(2,1)} %all-gather.2.cloned.1.call-done, bf16[1024,256]{1,0:T(8,128)(2,1)S(1)} %copy-done.8), kind=kOutput, calls=%fused_computation.43 | convolution fusion | flops 268566528 | bytes 1835008 | tf_op jit(solution)/shard_map/dot_general | solution.py:56
  68.4 1.1 convolution_convert_fusion.1
  69.6 1.1 convolution_convert_fusion.3
  70.8 23.4 %while.12 = (s32[]{:T(128)}, bf16[2,256,256]{2,1,0:T(8,128)(2,1)}, bf16[2,1024,256]{2,1,0:T(8,128)(2,1)S(1)}, bf16[2,256,256]{2,1,0:T(8,128)(2,1)}, s32[2]{0:T(1...) while((s32[]{:T(128)}, bf16[2,256,256]{2,1,0:T(8,128)(2,1)}, ...), condition=%wide.region_4.5_spmd, body=%wide.region_1.4_spmd.sunk | while | flops 521149696 | bytes 12803309 | solution.py:41
  70.8 0.6 dynamic_slice.59
  71.5 0.7 iota_compare_fusion.4
  72.1 0.2 fusion.76
  72.4 1.1 constant_dynamic-slice_fusion.9
  73.5 0.2 copy.40
  73.7 1.0 constant_dynamic-slice_fusion.10
  74.7 0.1 copy.38
  74.9 2.3 %fusion.77 = f32[4,256]{1,0:T(4,128)S(1)} fusion(pred[256,1280]{1,0:T(8,128)(4,1)S(1)} %fusion.76, bf16[256,4,64]{0,2,1:T(8,128)(2,1)S(1)} %bitcast.53, bf16[256,4,64]{0,2,1:T(8,128)(2,1)S(1)} %bitcast.55, bf16[1024,4,64]{0,2,1:T(8,128)(2,1)S(1)} %bitcast.50), kind=kOutput, calls=%fused_computation.7.clone.1 | convolution fusion | flops 175637760 | bytes 1118208 | tf_op jit(solution)/shard_map/while/body/eval_jaxpr/sub | solution.py:29
  77.3 0.2 copy.37
  77.5 0.9 constant_dynamic-slice_fusion.8
  78.5 3.1 %fusion.78 = bf16[256,4,64]{0,2,1:T(8,128)(2,1)S(1)} fusion(pred[256,1280]{1,0:T(8,128)(4,1)S(1)} %fusion.76, bf16[256,4,64]{0,2,1:T(8,128)(2,1)S(1)} %bitcast.57, bf16[1024,4,64]{0,2,1:T(8,128)(2,1)S(1)} %bitcast.52, bf16[256,4,64]{0,2,1:T(8,128)(2,1)} %bitcast.54, bf16[256,4,64]{0,2,1:T(8,128)(2,1)} %bitcast.56, ...), kind=kOutput, calls=%fused_computation.16.clone.1 | convolution fusion | flops 344852736 | bytes 1904640 | tf_op jit(solution)/shard_map/while/body/eval_jaxpr/hqk,khd->qhd/dot_general | solution.py:31
  81.7 0.1 copy.41
  81.8 0.7 copy-done.6
  82.5 0.6 dynamic_slice.59
  83.2 0.7 iota_compare_fusion.4
  83.9 0.2 fusion.76
  84.1 1.1 constant_dynamic-slice_fusion.9
  85.2 0.2 copy.40
  85.4 1.0 constant_dynamic-slice_fusion.10
  86.7 2.3 %fusion.77 = f32[4,256]{1,0:T(4,128)S(1)} fusion(pred[256,1280]{1,0:T(8,128)(4,1)S(1)} %fusion.76, bf16[256,4,64]{0,2,1:T(8,128)(2,1)S(1)} %bitcast.53, bf16[256,4,64]{0,2,1:T(8,128)(2,1)S(1)} %bitcast.55, bf16[1024,4,64]{0,2,1:T(8,128)(2,1)S(1)} %bitcast.50), kind=kOutput, calls=%fused_computation.7.clone.1 | convolution fusion | flops 175637760 | bytes 1118208 | tf_op jit(solution)/shard_map/while/body/eval_jaxpr/sub | solution.py:29
  89.0 0.2 copy.37
  89.2 0.9 constant_dynamic-slice_fusion.8
  90.3 3.1 %fusion.78 = bf16[256,4,64]{0,2,1:T(8,128)(2,1)S(1)} fusion(pred[256,1280]{1,0:T(8,128)(4,1)S(1)} %fusion.76, bf16[256,4,64]{0,2,1:T(8,128)(2,1)S(1)} %bitcast.57, bf16[1024,4,64]{0,2,1:T(8,128)(2,1)S(1)} %bitcast.52, bf16[256,4,64]{0,2,1:T(8,128)(2,1)} %bitcast.54, bf16[256,4,64]{0,2,1:T(8,128)(2,1)} %bitcast.56, ...), kind=kOutput, calls=%fused_computation.16.clone.1 | convolution fusion | flops 344852736 | bytes 1904640 | tf_op jit(solution)/shard_map/while/body/eval_jaxpr/hqk,khd->qhd/dot_general | solution.py:31
  93.4 0.1 copy.41
  93.5 0.7 copy-done.6
  94.2 2.4 %convolution_convert_fusion = bf16[512,1024]{1,0:T(8,128)(2,1)} fusion(bf16[512,256]{1,0:T(8,128)(2,1)} %bitcast.62, bf16[256,1024]{1,0:T(8,128)(2,1)S(1)} %copy-done), kind=kOutput, calls=%fused_computation.41 | convolution fusion | flops 268959744 | bytes 1835008 | tf_op jit(solution)/shard_map/dot_general | solution.py:64
  96.7 0.8 dynamic_slice.45
  97.4 0.8 dynamic_slice.46
  98.2 27.0 %reduce-scatter.2.cloned.1.call-done = bf16[512,256]{1,0:T(8,128)(2,1)} async-done(((bf16[512,1024]{1,0:T(8,128)(2,1)}), bf16[512,256]{1,0:T(8,128)(2,1)}) %reduce-scatter.2.cloned.1.call-update) | async-done | bytes 262160 | tf_op jit(solution)/shard_map/reduce_scatter | solution.py:65
  125.2 1.2 fusion.46
  126.4 10.6 %all-reduce = (f32[512]{0:T(512)S(1)}, f32[512]{0:T(512)S(1)}) all-reduce(f32[512]{0:T(512)S(1)} %get-tuple-element.124, f32[512]{0:T(512)S(1)} %get-tuple-element.123), channel_id=1, replica_groups=mesh['req'=128,'tp'=4] {'tp'}, use_global_device_ids=true, to_apply=%region_9.10 | all-reduce | flops 1024 | bytes 8192 | tf_op jit(solution)/shard_map/psum | solution.py:69
  137.0 1.2 add_convert_fusion
  138.2 0.8 reshape.149
  138.9 14.5 %all-to-all-start.1 = ((bf16[128,4,256]{2,1,0:T(4,128)(2,1)}), bf16[128,4,256]{2,1,0:T(4,128)(2,1)S(1)}, u32[]{:S(2)}, u32[]{:S(2)}) async-start(bf16[128,4,256]{2,1,0:T(4,128)(2,1)} %reshape.149), calls=%async_computation.2 | async-start | bytes 524288 | tf_op jit(solution)/shard_map/all_to_all | solution.py:105
  153.4 15.1 %all-to-all-done.1 = bf16[128,4,256]{2,1,0:T(4,128)(2,1)S(1)} async-done(((bf16[128,4,256]{2,1,0:T(4,128)(2,1)}), bf16[128,4,256]{2,1,0:T(4,128)(2,1)S(1)}, u32[]{:S(2)}, u32[]{:S(2)}) %all-to-all-start.1) | async-done | bytes 262176 | tf_op jit(solution)/shard_map/all_to_all | solution.py:105
  168.5 0.8 gather_fusion.1
  169.3 0.8 reshape.150
  (49 shorter events, 0.8 us)
Async XLA Ops:
  6.5 87.7 %copy-start = (bf16[256,1024]{1,0:T(8,128)(2,1)S(1)}, bf16[256,1024]{1,0:T(8,128)(2,1)}, u32[]{:S(2)}) copy-start(bf16[256,1024]{1,0:T(8,128)(2,1)} %param.19) | copy-start | bytes 1572868
  6.5 59.4 %all-gather.2.cloned.1.call-start = ((), (), s32[]{:S(2)}) async-start(), calls=%async_computation.3 | async-start | bytes 1310720 | tf_op jit(solution)/shard_map/all_gather | solution.py:101
  9.3 56.7 %copy-start.8 = (bf16[1024,256]{1,0:T(8,128)(2,1)S(1)}, bf16[1024,256]{1,0:T(8,128)(2,1)}, u32[]{:S(2)}) copy-start(bf16[1024,256]{1,0:T(8,128)(2,1)} %param.16) | copy-start | bytes 1572868
  43.6 24.8 %copy-start.9 = (bf16[1024,256]{1,0:T(8,128)(2,1)S(1)}, bf16[1024,256]{1,0:T(8,128)(2,1)}, u32[]{:S(2)}) copy-start(bf16[1024,256]{1,0:T(8,128)(2,1)} %param.17) | copy-start | bytes 1572868
  43.6 81.6 %reduce-scatter.2.cloned.1.call-start = ((), (), s32[]{:S(2)}) async-start(), calls=%async_computation.4 | async-start | bytes 1310720 | tf_op jit(solution)/shard_map/reduce_scatter | solution.py:65
  65.9 2.5 %copy-start.7 = (bf16[512,1024]{1,0:T(8,128)(2,1)S(1)}, bf16[512,1024]{1,0:T(8,128)(2,1)}, u32[]{:S(2)}) copy-start(bf16[512,1024]{1,0:T(8,128)(2,1)} %all-gather.2.cloned.1.call-done) | copy-start | bytes 3145732
  68.4 1.1 copy-start.10
  69.6 1.2 copy-start.1
  69.6 1.2 copy-start.11
  74.8 2.5 %copy-start.3 = (bf16[1,256,256]{1,2,0:T(8,128)(2,1)}, bf16[1,256,256]{1,2,0:T(8,128)(2,1)S(1)}, u32[]{:S(2)}) copy-start(bf16[1,256,256]{1,2,0:T(8,128)(2,1)S(1)} %copy.38) | copy-start | bytes 393220 | tf_op jit(solution)/shard_map/while
  74.9 2.3 %copy-start.4 = (bf16[1,256,256]{1,2,0:T(8,128)(2,1)}, bf16[1,256,256]{1,2,0:T(8,128)(2,1)S(1)}, u32[]{:S(2)}) copy-start(bf16[1,256,256]{1,2,0:T(8,128)(2,1)S(1)} %copy.39) | copy-start | bytes 393220 | tf_op jit(solution)/shard_map/while
  78.5 3.3 %copy-start.5 = (bf16[2,256,256]{2,1,0:T(8,128)(2,1)S(1)}, bf16[2,256,256]{2,1,0:T(8,128)(2,1)}, u32[]{:S(2)}) copy-start(bf16[2,256,256]{2,1,0:T(8,128)(2,1)} %get-tuple-element.222) | copy-start | bytes 786436 | tf_op jit(solution)/shard_map/while
  81.8 0.7 copy-start.6
  86.5 2.5 %copy-start.3 = (bf16[1,256,256]{1,2,0:T(8,128)(2,1)}, bf16[1,256,256]{1,2,0:T(8,128)(2,1)S(1)}, u32[]{:S(2)}) copy-start(bf16[1,256,256]{1,2,0:T(8,128)(2,1)S(1)} %copy.38) | copy-start | bytes 393220 | tf_op jit(solution)/shard_map/while
  86.6 2.3 %copy-start.4 = (bf16[1,256,256]{1,2,0:T(8,128)(2,1)}, bf16[1,256,256]{1,2,0:T(8,128)(2,1)S(1)}, u32[]{:S(2)}) copy-start(bf16[1,256,256]{1,2,0:T(8,128)(2,1)S(1)} %copy.39) | copy-start | bytes 393220 | tf_op jit(solution)/shard_map/while
  90.2 3.3 %copy-start.5 = (bf16[2,256,256]{2,1,0:T(8,128)(2,1)S(1)}, bf16[2,256,256]{2,1,0:T(8,128)(2,1)}, u32[]{:S(2)}) copy-start(bf16[2,256,256]{2,1,0:T(8,128)(2,1)} %get-tuple-element.222) | copy-start | bytes 786436 | tf_op jit(solution)/shard_map/while
  93.5 0.7 copy-start.6
  94.2 31.0 %copy-start.2 = (bf16[512,256]{1,0:T(8,128)(2,1)S(1)}, bf16[512,256]{1,0:T(8,128)(2,1)}, u32[]{:S(2)}) copy-start(bf16[512,256]{1,0:T(8,128)(2,1)} %reshape.144) | copy-start | bytes 786436
  138.9 29.6 %all-to-all-start.1 = ((bf16[128,4,256]{2,1,0:T(4,128)(2,1)}), bf16[128,4,256]{2,1,0:T(4,128)(2,1)S(1)}, u32[]{:S(2)}, u32[]{:S(2)}) async-start(bf16[128,4,256]{2,1,0:T(4,128)(2,1)} %reshape.149), calls=%async_computation.2 | async-start | bytes 524288 | tf_op jit(solution)/shard_map/all_to_all | solution.py:105
Sparse Core Ops, SparseCore 0:
  43.7 22.1 all-gather.1
  96.8 28.3 reduce-scatter.1
where the time goes:
time: 178 us; the launch traced here: 177 us
  waiting for transfers between devices  64.4 us (36%)
  blocking collectives  43.3 us (24%)
  matrix products  18.1 us (10%)
  local copies, waits for them, and re-layouts  18 us (10%)
  starting transfers between devices  14.5 us (8%)
  between operations  13.5 us (8%)
  other arithmetic  4.9 us (3%)
    all_to_all x1, blocking collectives, shards(): lax.all_to_all(to_blocks(tokens)[send_order], 'req', split_axis=0, concat...  32.7 us
    reduce_scatter x1, waiting for transfers between devices, finish_rows(): lax.psum_scatter(partial_sum.astype(jnp.bfloat16), 'tp', scatter_dimensio...  27 us
    all_gather x1, waiting for transfers between devices, shards(): whole = lax.all_gather(arrived, 'tp', axis=1, tiled=True)  22.3 us
    all_to_all x1, waiting for transfers between devices, shards(): lax.all_to_all(to_blocks(normed), 'req', split_axis=0, concat_axis=0, til...  15.1 us
    all_to_all x1, starting transfers between devices, shards(): lax.all_to_all(to_blocks(normed), 'req', split_axis=0, concat_axis=0, til...  14.5 us
    psum x1, blocking collectives, finish_rows(): lax.psum((jnp.sum(summed, axis=1), jnp.sum(summed * summed, axis=1)), 'tp')  10.6 us
    dynamic_slice x18, local copies, waits for them, and re-layouts, attend_all(): lax.map(lambda items: attend_padded(*items), (queries.reshape(req_shape),...  8.77 us
    dot_general x2, matrix products, attend_padded(): jnp.einsum('hqk,khd->qhd', weight.astype(jnp.bfloat16), values_all, prefe...  6.26 us
  transfers between devices with their start and end apart: 3, of which 3 were waited for; matrix products, arithmetic and copies ran while one was open for 1% of the time, Pallas kernels for 0%

commit v1 on v0

--- a/solution.py
+++ b/solution.py
@@ -98,7 +98,16 @@
     arrived = lax.all_to_all(
         to_blocks(tokens)[send_order], "req", split_axis=0, concat_axis=0, tiled=True
     ).reshape(row_count, feat_width)
-    whole = lax.all_gather(arrived, "tp", axis=1, tiled=True)
+    area_launch = lambda point, bus_axis: jnp.concatenate(
+        lax.all_to_all(
+            jnp.stack([point] * lax.axis_size(bus_axis), 0),
+            axis_name=bus_axis,
+            split_axis=0,
+            concat_axis=0,
+        ),
+        1,
+    )
+    whole = area_launch(arrived, "tp")
     queries, new_keys, new_values = project_rows(whole, w_query, w_key, w_value)
     context = attend_all(queries, new_keys, new_values, k_cache, v_cache, cache_len)
     normed = finish_rows(context, arrived, w_out, ln_gain, ln_bias)

time: 178 us -> 163 us (0.916)
  waiting for transfers between devices: 64.4 us -> 45.4 us
  starting transfers between devices: 14.5 us -> 19.5 us
    all_gather x1 -> x0, waiting for transfers between devices: 22.3 us -> none  [shards(): whole = lax.all_gather(arrived, 'tp', axis=1, tiled=True)]
    all_to_all x0 -> x1, waiting for transfers between devices: none -> 12.6 us  [shards(): lax.all_to_all(jnp.stack([point] * lax.axis_size(bus_axis), 0), axis_name...]
    reduce_scatter x1, waiting for transfers between devices: 27 us -> 17.7 us  [finish_rows(): lax.psum_scatter(partial_sum.astype(jnp.bfloat16), 'tp', scatter_dimensio...]
    all_to_all x0 -> x1, starting transfers between devices: none -> 4.96 us  [shards(): lax.all_to_all(jnp.stack([point] * lax.axis_size(bus_axis), 0), axis_name...]
where the time goes in v1:
time: 163 us; the launch traced here: 162 us
  waiting for transfers between devices  45.4 us (28%)
  blocking collectives  43.3 us (27%)
  starting transfers between devices  19.5 us (12%)
  local copies, waits for them, and re-layouts  18.4 us (11%)
  matrix products  16.8 us (10%)
  between operations  13.5 us (8%)
  other arithmetic  4.82 us (3%)
    all_to_all x1, blocking collectives, shards(): lax.all_to_all(to_blocks(tokens)[send_order], 'req', split_axis=0, concat...  32.7 us
    reduce_scatter x1, waiting for transfers between devices, finish_rows(): lax.psum_scatter(partial_sum.astype(jnp.bfloat16), 'tp', scatter_dimensio...  17.7 us
    all_to_all x1, waiting for transfers between devices, shards(): lax.all_to_all(to_blocks(normed), 'req', split_axis=0, concat_axis=0, til...  15.1 us
    all_to_all x1, starting transfers between devices, shards(): lax.all_to_all(to_blocks(normed), 'req', split_axis=0, concat_axis=0, til...  14.5 us
    all_to_all x1, waiting for transfers between devices, shards(): lax.all_to_all(jnp.stack([point] * lax.axis_size(bus_axis), 0), axis_name...  12.6 us
    psum x1, blocking collectives, finish_rows(): lax.psum((jnp.sum(summed, axis=1), jnp.sum(summed * summed, axis=1)), 'tp')  10.6 us
    dynamic_slice x18, local copies, waits for them, and re-layouts, attend_all(): lax.map(lambda items: attend_padded(*items), (queries.reshape(req_shape),...  8.68 us
    dot_general x2, matrix products, attend_padded(): jnp.einsum('hqk,khd->qhd', weight.astype(jnp.bfloat16), values_all, prefe...  6.26 us
  transfers between devices with their start and end apart: 3, of which 3 were waited for; matrix products, arithmetic and copies ran while one was open for 1% of the time, Pallas kernels for 0%

profile of v1, /device:TPU:2, one launch (start us, length us, event | category | flops | bytes accessed | tf_op | source)
XLA Modules:
  0.0 162.0 jit_solution(3553267485561983643)
XLA Ops:
  6.5 0.7 compare_select_fusion.1
  7.3 1.0 scatter_custom_fusion
  8.3 1.0 reshape.151
  9.3 0.8 gather_fusion
  10.1 32.7 %all_to_all.15 = bf16[128,4,256]{2,1,0:T(4,128)(2,1)S(1)} all-to-all(bf16[128,4,256]{2,1,0:T(4,128)(2,1)S(1)} %gather_fusion), channel_id=1, replica_groups=mesh['req'=128,'tp'=4] {'req'}, dimensions={0} | all-to-all | bytes 524288 | tf_op jit(solution)/shard_map/all_to_all | solution.py:98
  42.9 0.1 copy.17
  43.1 1.0 stack.3
  44.1 5.0 %all-to-all-start.1 = ((bf16[4,512,256]{1,2,0:T(8,128)(2,1)}), bf16[4,512,256]{1,2,0:T(8,128)(2,1)S(1)}, u32[]{:S(2)}, u32[]{:S(2)}) async-start(bf16[4,512,256]{1,2,0:T(8,128)(2,1)} %stack.3), calls=%async_computation.1 | async-start | bytes 2097152 | tf_op jit(solution)/shard_map/all_to_all | solution.py:102
  49.1 12.6 %all-to-all-done.1 = bf16[4,512,256]{1,2,0:T(8,128)(2,1)S(1)} async-done(((bf16[4,512,256]{1,2,0:T(8,128)(2,1)}), bf16[4,512,256]{1,2,0:T(8,128)(2,1)S(1)}, u32[]{:S(2)}, u32[]{:S(2)}) %all-to-all-start.1) | async-done | bytes 1048608 | tf_op jit(solution)/shard_map/all_to_all | solution.py:102
  61.7 1.2 convolution_convert_fusion.3
  62.9 1.2 convolution_convert_fusion.2
  64.1 1.2 convolution_convert_fusion.1
  65.3 23.3 %while.12 = (s32[]{:T(128)}, bf16[2,256,256]{2,1,0:T(8,128)(2,1)}, bf16[2,1024,256]{2,1,0:T(8,128)(2,1)S(1)}, bf16[2,256,256]{2,1,0:T(8,128)(2,1)}, s32[2]{0:T(1...) while((s32[]{:T(128)}, bf16[2,256,256]{2,1,0:T(8,128)(2,1)}, ...), condition=%wide.region_4.5_spmd, body=%wide.region_1.4_spmd.sunk | while | flops 521149696 | bytes 12803309 | solution.py:41
  65.3 0.6 dynamic_slice.59
  65.9 0.6 iota_compare_fusion.4
  66.6 0.2 fusion.76
  66.8 1.1 constant_dynamic-slice_fusion.9
  67.9 0.2 copy.41
  68.1 1.0 constant_dynamic-slice_fusion.10
  69.4 2.3 %fusion.77 = f32[4,256]{1,0:T(4,128)S(1)} fusion(pred[256,1280]{1,0:T(8,128)(4,1)S(1)} %fusion.76, bf16[256,4,64]{0,2,1:T(8,128)(2,1)S(1)} %bitcast.56, bf16[256,4,64]{0,2,1:T(8,128)(2,1)S(1)} %bitcast.58, bf16[1024,4,64]{0,2,1:T(8,128)(2,1)S(1)} %bitcast.53), kind=kOutput, calls=%fused_computation.7.clone.1 | convolution fusion | flops 175637760 | bytes 1118208 | tf_op jit(solution)/shard_map/while/body/eval_jaxpr/sub | solution.py:29
  71.7 0.2 copy.38
  71.9 0.9 constant_dynamic-slice_fusion.8
  73.0 3.1 %fusion.78 = bf16[256,4,64]{0,2,1:T(8,128)(2,1)S(1)} fusion(pred[256,1280]{1,0:T(8,128)(4,1)S(1)} %fusion.76, bf16[256,4,64]{0,2,1:T(8,128)(2,1)S(1)} %bitcast.60, bf16[1024,4,64]{0,2,1:T(8,128)(2,1)S(1)} %bitcast.55, bf16[256,4,64]{0,2,1:T(8,128)(2,1)} %bitcast.57, bf16[256,4,64]{0,2,1:T(8,128)(2,1)} %bitcast.59, ...), kind=kOutput, calls=%fused_computation.16.clone.1 | convolution fusion | flops 344852736 | bytes 1904640 | tf_op jit(solution)/shard_map/while/body/eval_jaxpr/hqk,khd->qhd/dot_general | solution.py:31
  76.2 0.7 copy-done.7
  76.9 0.6 dynamic_slice.59
  77.5 0.6 iota_compare_fusion.4
  78.2 0.2 fusion.76
  78.4 1.1 constant_dynamic-slice_fusion.9
  79.6 0.2 copy.41
  79.8 1.0 constant_dynamic-slice_fusion.10
  81.0 2.3 %fusion.77 = f32[4,256]{1,0:T(4,128)S(1)} fusion(pred[256,1280]{1,0:T(8,128)(4,1)S(1)} %fusion.76, bf16[256,4,64]{0,2,1:T(8,128)(2,1)S(1)} %bitcast.56, bf16[256,4,64]{0,2,1:T(8,128)(2,1)S(1)} %bitcast.58, bf16[1024,4,64]{0,2,1:T(8,128)(2,1)S(1)} %bitcast.53), kind=kOutput, calls=%fused_computation.7.clone.1 | convolution fusion | flops 175637760 | bytes 1118208 | tf_op jit(solution)/shard_map/while/body/eval_jaxpr/sub | solution.py:29
  83.3 0.2 copy.38
  83.6 0.9 constant_dynamic-slice_fusion.8
  84.6 3.1 %fusion.78 = bf16[256,4,64]{0,2,1:T(8,128)(2,1)S(1)} fusion(pred[256,1280]{1,0:T(8,128)(4,1)S(1)} %fusion.76, bf16[256,4,64]{0,2,1:T(8,128)(2,1)S(1)} %bitcast.60, bf16[1024,4,64]{0,2,1:T(8,128)(2,1)S(1)} %bitcast.55, bf16[256,4,64]{0,2,1:T(8,128)(2,1)} %bitcast.57, bf16[256,4,64]{0,2,1:T(8,128)(2,1)} %bitcast.59, ...), kind=kOutput, calls=%fused_computation.16.clone.1 | convolution fusion | flops 344852736 | bytes 1904640 | tf_op jit(solution)/shard_map/while/body/eval_jaxpr/hqk,khd->qhd/dot_general | solution.py:31
  87.7 0.1 copy.42
  87.9 0.7 copy-done.7
  88.6 2.4 %convolution_convert_fusion = bf16[512,1024]{1,0:T(8,128)(2,1)} fusion(bf16[512,256]{1,0:T(8,128)(2,1)} %bitcast.68, bf16[256,1024]{1,0:T(8,128)(2,1)S(1)} %copy-done), kind=kOutput, calls=%fused_computation.41 | convolution fusion | flops 268959744 | bytes 1835008 | tf_op jit(solution)/shard_map/dot_general | solution.py:64
  91.0 0.8 dynamic_slice.45
  91.8 0.8 dynamic_slice.46
  92.5 17.7 %reduce-scatter.2.cloned.1.call-done = bf16[512,256]{1,0:T(8,128)(2,1)} async-done(((bf16[512,1024]{1,0:T(8,128)(2,1)}), bf16[512,256]{1,0:T(8,128)(2,1)}) %reduce-scatter.2.cloned.1.call-update) | async-done | bytes 262160 | tf_op jit(solution)/shard_map/reduce_scatter | solution.py:65
  110.2 1.2 fusion.46
  111.4 10.6 %all-reduce = (f32[512]{0:T(512)S(1)}, f32[512]{0:T(512)S(1)}) all-reduce(f32[512]{0:T(512)S(1)} %get-tuple-element.124, f32[512]{0:T(512)S(1)} %get-tuple-element.123), channel_id=1, replica_groups=mesh['req'=128,'tp'=4] {'tp'}, use_global_device_ids=true, to_apply=%region_9.10 | all-reduce | flops 1024 | bytes 8192 | tf_op jit(solution)/shard_map/psum | solution.py:69
  122.0 1.2 add_convert_fusion
  123.2 0.8 reshape.159
  124.0 14.5 %all-to-all-start.2 = ((bf16[128,4,256]{2,1,0:T(4,128)(2,1)}), bf16[128,4,256]{2,1,0:T(4,128)(2,1)S(1)}, u32[]{:S(2)}, u32[]{:S(2)}) async-start(bf16[128,4,256]{2,1,0:T(4,128)(2,1)} %reshape.159), calls=%async_computation.3 | async-start | bytes 524288 | tf_op jit(solution)/shard_map/all_to_all | solution.py:114
  138.5 15.1 %all-to-all-done.2 = bf16[128,4,256]{2,1,0:T(4,128)(2,1)S(1)} async-done(((bf16[128,4,256]{2,1,0:T(4,128)(2,1)}), bf16[128,4,256]{2,1,0:T(4,128)(2,1)S(1)}, u32[]{:S(2)}, u32[]{:S(2)}) %all-to-all-start.2) | async-done | bytes 262176 | tf_op jit(solution)/shard_map/all_to_all | solution.py:114
  153.6 0.8 gather_fusion.1
  154.4 0.8 reshape.160
  (50 shorter events, 1.0 us)
Async XLA Ops:
  6.5 82.0 %copy-start = (bf16[256,1024]{1,0:T(8,128)(2,1)S(1)}, bf16[256,1024]{1,0:T(8,128)(2,1)}, u32[]{:S(2)}) copy-start(bf16[256,1024]{1,0:T(8,128)(2,1)} %param.19) | copy-start | bytes 1572868
  42.9 1.2 copy-start.2
  44.1 17.6 %copy-start.8 = (bf16[1024,256]{1,0:T(8,128)(2,1)S(1)}, bf16[1024,256]{1,0:T(8,128)(2,1)}, u32[]{:S(2)}) copy-start(bf16[1024,256]{1,0:T(8,128)(2,1)} %param.18) | copy-start | bytes 1572868
  44.1 17.6 %all-to-all-start.1 = ((bf16[4,512,256]{1,2,0:T(8,128)(2,1)}), bf16[4,512,256]{1,2,0:T(8,128)(2,1)S(1)}, u32[]{:S(2)}, u32[]{:S(2)}) async-start(bf16[4,512,256]{1,2,0:T(8,128)(2,1)} %stack.3), calls=%async_computation.1 | async-start | bytes 2097152 | tf_op jit(solution)/shard_map/all_to_all | solution.py:102
  49.1 61.2 %reduce-scatter.2.cloned.1.call-start = ((), (), s32[]{:S(2)}) async-start(), calls=%async_computation.4 | async-start | bytes 1310720 | tf_op jit(solution)/shard_map/reduce_scatter | solution.py:65
  61.7 1.2 copy-start.9
  62.9 1.2 copy-start.10
  64.1 1.2 copy-start.1
  64.1 1.2 copy-start.11
  69.2 2.5 %copy-start.4 = (bf16[1,256,256]{1,2,0:T(8,128)(2,1)}, bf16[1,256,256]{1,2,0:T(8,128)(2,1)S(1)}, u32[]{:S(2)}) copy-start(bf16[1,256,256]{1,2,0:T(8,128)(2,1)S(1)} %copy.39) | copy-start | bytes 393220 | tf_op jit(solution)/shard_map/while
  69.3 2.3 %copy-start.5 = (bf16[1,256,256]{1,2,0:T(8,128)(2,1)}, bf16[1,256,256]{1,2,0:T(8,128)(2,1)S(1)}, u32[]{:S(2)}) copy-start(bf16[1,256,256]{1,2,0:T(8,128)(2,1)S(1)} %copy.40) | copy-start | bytes 393220 | tf_op jit(solution)/shard_map/while
  72.9 3.3 %copy-start.6 = (bf16[2,256,256]{2,1,0:T(8,128)(2,1)S(1)}, bf16[2,256,256]{2,1,0:T(8,128)(2,1)}, u32[]{:S(2)}) copy-start(bf16[2,256,256]{2,1,0:T(8,128)(2,1)} %get-tuple-element.222) | copy-start | bytes 786436 | tf_op jit(solution)/shard_map/while
  76.2 0.7 copy-start.7
  80.9 2.5 %copy-start.4 = (bf16[1,256,256]{1,2,0:T(8,128)(2,1)}, bf16[1,256,256]{1,2,0:T(8,128)(2,1)S(1)}, u32[]{:S(2)}) copy-start(bf16[1,256,256]{1,2,0:T(8,128)(2,1)S(1)} %copy.39) | copy-start | bytes 393220 | tf_op jit(solution)/shard_map/while
  81.0 2.3 %copy-start.5 = (bf16[1,256,256]{1,2,0:T(8,128)(2,1)}, bf16[1,256,256]{1,2,0:T(8,128)(2,1)S(1)}, u32[]{:S(2)}) copy-start(bf16[1,256,256]{1,2,0:T(8,128)(2,1)S(1)} %copy.40) | copy-start | bytes 393220 | tf_op jit(solution)/shard_map/while
  84.6 3.3 %copy-start.6 = (bf16[2,256,256]{2,1,0:T(8,128)(2,1)S(1)}, bf16[2,256,256]{2,1,0:T(8,128)(2,1)}, u32[]{:S(2)}) copy-start(bf16[2,256,256]{2,1,0:T(8,128)(2,1)} %get-tuple-element.222) | copy-start | bytes 786436 | tf_op jit(solution)/shard_map/while
  87.9 0.7 copy-start.7
  88.6 21.7 %copy-start.3 = (bf16[512,256]{1,0:T(8,128)(2,1)S(1)}, bf16[512,256]{1,0:T(8,128)(2,1)}, u32[]{:S(2)}) copy-start(bf16[512,256]{1,0:T(8,128)(2,1)} %copy-done.2) | copy-start | bytes 786436
  124.0 29.6 %all-to-all-start.2 = ((bf16[128,4,256]{2,1,0:T(4,128)(2,1)}), bf16[128,4,256]{2,1,0:T(4,128)(2,1)S(1)}, u32[]{:S(2)}, u32[]{:S(2)}) async-start(bf16[128,4,256]{2,1,0:T(4,128)(2,1)} %reshape.159), calls=%async_computation.3 | async-start | bytes 524288 | tf_op jit(solution)/shard_map/all_to_all | solution.py:114
Sparse Core Ops, SparseCore 0:
  91.1 19.0 reduce-scatter.1
